TPU v7x, 32 devices: a whole 2x2x4 slice. The times are simulated.
32 devices in a mesh: section: 4 (over y, core), expert: 8 (over z, x).
Axes of the slice: x: 2, y: 2, z: 4, core: 2. Of those that a mesh axis runs over, the one named last changes fastest.
Arguments:
- upstream: bfloat16 [4, 1024, 2048], P('section', 'expert'), may hold values from -6 to 6
- layer_input: bfloat16 [4, 1024, 2048], P('section', 'expert'), may hold values from -6 to 6
- routes: int32 [4, 1024, 2], P('section', 'expert'), may hold values from 0 to 3, all different within a row; in each aligned block of 128 rows (0 to 127, 128 to 255, ..., all dimensions but the last counted through in order) at most 128 rows name the same one
- gate_units: int32 [4, 1024, 2], P('section', 'expert'), may hold values from 1 to 256
- gate_weight: bfloat16 [4, 2048, 3072], P('section', None, 'expert'), may hold values from -0.125 to 0.125
- up_weight: bfloat16 [4, 2048, 3072], P('section', None, 'expert'), may hold values from -0.125 to 0.125
- down_weight: bfloat16 [4, 3072, 2048], P('section', 'expert'), may hold values from -0.21875 to 0.21875
Outputs:
- grad_input: bfloat16 [4, 1024, 2048], P('section', 'expert')
- grad_gate: bfloat16 [4, 2048, 3072], P('section', None, 'expert')
- grad_up: bfloat16 [4, 2048, 3072], P('section', None, 'expert')
- grad_down: bfloat16 [4, 3072, 2048], P('section', 'expert')
Inputs may be any that keep to these rules, and one draw needn't show every extreme that they name: `routes`: each token names 2 different experts; in each block of 128 tokens of a section (the tokens of one device) at most 128 tokens name one expert, and in some block exactly 128 do.
All inputs are finite; a program needn't handle non-finite values.
Results may differ from a plain program's by a relative error of at most 0.0058.
Values may be sent and summed in bfloat16 or wider, within the bound.
No kernel may reach another device: no remote copies, remote signals or barrier semaphores. Data moves between devices by JAX's collectives and lax.ppermute only.
A program may use at most 128 MiB of HBM per device.

v0:
```python
import jax
import jax.numpy as jnp
from jax import lax
from jax.sharding import PartitionSpec as P


def passed_along(value, axis, steps):
    count = lax.axis_size(axis)
    pairs = [(source, (source + steps) % count) for source in range(count)]
    return lax.ppermute(value, axis, pairs)


def expert_half(inputs, grads, w_gate, w_up, w_down):
    gate = jnp.dot(inputs, w_gate, preferred_element_type=jnp.float32)
    upper = jnp.dot(inputs, w_up, preferred_element_type=jnp.float32)
    sig = jax.nn.sigmoid(gate)
    act = gate * sig
    hidden = (act * upper).astype(jnp.bfloat16)
    dact = lax.dot_general(
        grads, w_down, (((1,), (1,)), ((), ())), preferred_element_type=jnp.float32
    )
    d_up = (dact * act).astype(jnp.bfloat16)
    d_gate = (dact * upper * sig * (1.0 + gate * (1.0 - sig))).astype(jnp.bfloat16)
    inner = (((1,), (1,)), ((), ()))
    d_in = lax.dot_general(d_gate, w_gate, inner, preferred_element_type=jnp.float32)
    d_in = d_in + lax.dot_general(d_up, w_up, inner, preferred_element_type=jnp.float32)
    outer = (((0,), (0,)), ((), ()))
    g_down = lax.dot_general(hidden, grads, outer, preferred_element_type=jnp.float32).astype(
        jnp.bfloat16
    )
    g_gate = lax.dot_general(inputs, d_gate, outer, preferred_element_type=jnp.float32).astype(
        jnp.bfloat16
    )
    g_up = lax.dot_general(inputs, d_up, outer, preferred_element_type=jnp.float32).astype(
        jnp.bfloat16
    )
    return (d_in.astype(jnp.bfloat16), g_gate, g_up, g_down)


def shards(upstream, layer_input, routes, gate_units, gate_weight, up_weight, down_weight):
    received = passed_along(upstream, "section", -1)[0]
    tokens = layer_input[0]
    expert = lax.axis_index("expert") // 2
    all_tokens = lax.all_gather(tokens, "expert", axis=0, tiled=True)
    all_grads = lax.all_gather(received, "expert", axis=0, tiled=True)
    all_routes = lax.all_gather(routes[0], "expert", axis=0, tiled=True)
    all_units = lax.all_gather(gate_units[0], "expert", axis=0, tiled=True)
    gains = jnp.sum(
        jnp.where(all_routes == expert, all_units.astype(jnp.float32) / 256.0, 0.0), axis=1
    )
    weighted = (gains[:, None] * all_grads.astype(jnp.float32)).astype(jnp.bfloat16)
    d_in, g_gate, g_up, g_down = expert_half(
        all_tokens, weighted, gate_weight[0], up_weight[0], down_weight[0]
    )
    summed = lax.psum_scatter(d_in.astype(jnp.float32), "expert", scatter_dimension=0, tiled=True)
    grad_input = (summed + received.astype(jnp.float32)).astype(jnp.bfloat16)
    return (grad_input[None], g_gate[None], g_up[None], g_down[None])


def solution(mesh):
    in_specs = (
        P("section", "expert", None),
        P("section", "expert", None),
        P("section", "expert", None),
        P("section", "expert", None),
        P("section", None, "expert"),
        P("section", None, "expert"),
        P("section", "expert", None),
    )
    out_specs = (
        P("section", "expert", None),
        P("section", None, "expert"),
        P("section", None, "expert"),
        P("section", "expert", None),
    )
    return jax.shard_map(shards, mesh=mesh, in_specs=in_specs, out_specs=out_specs, check_vma=False)
```

profile of v0, /device:TPU:0, one launch (start us, length us, event | category | flops | bytes accessed | tf_op | source)
XLA Modules:
  0.0 331.4 jit_solution(4760866613073092125)
XLA Ops:
  7.2 0.0 copy-start
  7.2 0.0 all-gather.9.cloned.1.call-start
  7.2 0.7 all-gather.9.cloned.1.call-update
  7.9 0.0 all-gather.7.cloned.1.call-start
  8.0 2.5 collective-permute-start
  10.4 7.0 %collective-permute-done = bf16[1,128,2048]{2,1,0:T(8,128)(2,1)S(1)} collective-permute-done((bf16[1,128,2048]{2,1,0:T(8,128)(2,1)}, bf16[1,128,2048]{2,1,0:T(8,128)(2,1)S(1)}, u32[]{:S(2)}, u32[]{:S(2)}) %collective-permute-start) | collective-permute-done | bytes 524320 | tf_op jit(solution)/shard_map/ppermute | solution.py:10
  17.4 0.8 copy-done.1
  18.2 0.0 all-gather.7.cloned.1.call-update
  18.3 0.0 reduce-scatter.2.cloned.1.call-start
  18.3 21.2 %all-gather = s32[1,1024,2]{1,2,0:T(2,128)S(1)} all-gather(s32[1,128,2]{1,2,0:T(2,128)} %param.9), channel_id=2, replica_groups=mesh['section'=4,'expert'=8] {'expert'}, dimensions={1}, use_global_device_ids=true | all-gather | bytes 9216 | tf_op jit(solution)/shard_map/all_gather | solution.py:46
  39.6 16.8 %all-gather.1 = s32[1,1024,2]{1,2,0:T(2,128)S(1)} all-gather(s32[1,128,2]{1,2,0:T(2,128)} %param.10), channel_id=3, replica_groups=mesh['section'=4,'expert'=8] {'expert'}, dimensions={1}, use_global_device_ids=true | all-gather | bytes 9216 | tf_op jit(solution)/shard_map/all_gather | solution.py:47
  56.4 0.0 copy-start.3
  56.4 30.0 %all-gather.9.cloned.1.call-done = bf16[1,1024,2048]{2,1,0:T(8,128)(2,1)} async-done(((bf16[1,128,2048]{2,1,0:T(8,128)(2,1)}), bf16[1,1024,2048]{2,1,0:T(8,128)(2,1)}) %all-gather.9.cloned.1.call-update) | async-done | bytes 4194320 | tf_op jit(solution)/shard_map/all_gather | solution.py:44
  86.4 0.0 copy-done
  86.4 5.8 %fusion.5 = f32[1024,384]{1,0:T(8,128)} fusion(bf16[1,1024,2048]{2,1,0:T(8,128)(2,1)} %all-gather.9.cloned.1.call-done, bf16[1,2048,384]{2,1,0:T(8,128)(2,1)S(1)} %copy-done), kind=kOutput, calls=%fused_computation.7 | convolution fusion | flops 1610612736 | bytes 7340032 | tf_op jit(solution)/shard_map/dot_general | solution.py:14
  92.2 0.0 copy-done.3
  92.2 0.0 copy-done.6
  92.2 3.5 %fusion.7 = f32[1024,384]{1,0:T(8,128)} fusion(bf16[1,1024,2048]{2,1,0:T(8,128)(2,1)S(1)} %copy-done.6, bf16[1,2048,384]{2,1,0:T(8,128)(2,1)S(1)} %copy-done.3), kind=kOutput, calls=%fused_computation.9 | convolution fusion | flops 1610612736 | bytes 7340032 | tf_op jit(solution)/shard_map/dot_general | solution.py:15
  95.7 65.1 %all-gather.7.cloned.1.call-done = bf16[1,1024,2048]{2,1,0:T(8,128)(2,1)} async-done(((bf16[1,128,2048]{2,1,0:T(8,128)(2,1)}), bf16[1,1024,2048]{2,1,0:T(8,128)(2,1)}) %all-gather.7.cloned.1.call-update) | async-done | bytes 4194320 | tf_op jit(solution)/shard_map/all_gather | solution.py:45
  160.8 6.4 %multiply_convert_fusion.1 = (bf16[1024,384]{1,0:T(8,128)(2,1)S(1)}, bf16[1024,384]{1,0:T(8,128)(2,1)S(1)}) fusion(f32[1024,384]{1,0:T(8,128)} %fusion.5, f32[1024,384]{1,0:T(8,128)} %fusion.7, bf16[1,384,2048]{2,1,0:T(8,128)(2,1)} %param.13, bf16[1,1024,2048]{2,1,0:T(8,128)(2,1)} %all-gather.7.cloned.1.call-done, f32[1024]{0:T(1024)S(1)} %fusion.36), kind=kOutput, calls=%fused_computation.26 | convolution fusion | flops 1622016000 | bytes 10489856 | tf_op jit(solution)/shard_map/dot_general | solution.py:19
  167.2 0.0 copy-start.4
  167.2 0.0 copy-start.5
  167.2 2.4 fusion.26
  169.6 5.6 %fusion.9 = f32[1024,2048]{1,0:T(8,128)} fusion(f32[1024,2048]{1,0:T(8,128)S(1)} %fusion.26, bf16[1024,384]{1,0:T(8,128)(2,1)S(1)} %get-tuple-element.8, bf16[1,2048,384]{2,1,0:T(8,128)(2,1)S(1)} %copy-done.3), kind=kOutput, calls=%fused_computation.11 | convolution fusion | flops 1616904192 | bytes 19136512 | tf_op jit(solution)/shard_map/dot_general | solution.py:26
  175.2 0.0 reduce-scatter.2.cloned.1.call-update
  175.2 4.3 %fusion.20 = bf16[1,2048,384]{1,2,0:T(8,128)(2,1)S(1)} fusion(bf16[1024,384]{1,0:T(8,128)(2,1)} %copy-done.4, bf16[1,1024,2048]{2,1,0:T(8,128)(2,1)} %all-gather.9.cloned.1.call-done), kind=kOutput, calls=%fused_computation.17 | convolution fusion | flops 1611399168 | bytes 6553600 | tf_op jit(solution)/shard_map/dot_general | solution.py:31
  179.5 1.8 copy.11
  181.3 4.3 %fusion.17 = bf16[1,2048,384]{1,2,0:T(8,128)(2,1)S(1)} fusion(bf16[1024,384]{1,0:T(8,128)(2,1)} %copy-done.5, bf16[1,1024,2048]{2,1,0:T(8,128)(2,1)} %all-gather.9.cloned.1.call-done), kind=kOutput, calls=%fused_computation.16 | convolution fusion | flops 1611399168 | bytes 6553600 | tf_op jit(solution)/shard_map/dot_general | solution.py:34
  185.6 1.6 copy.12
  187.1 6.5 %fusion.16 = bf16[1,384,2048]{2,1,0:T(8,128)(2,1)} fusion(bf16[1,1024,2048]{2,1,0:T(8,128)(2,1)} %all-gather.7.cloned.1.call-done, f32[1024]{0:T(1024)S(1)} %fusion.36, f32[1024,384]{1,0:T(8,128)} %fusion.7, f32[1024,384]{1,0:T(8,128)} %fusion.5), kind=kOutput, calls=%fused_computation.15 | convolution fusion | flops 1620049920 | bytes 8916992 | tf_op jit(solution)/shard_map/dot_general | solution.py:28
  193.6 129.1 %reduce-scatter.2.cloned.1.call-done = f32[128,2048]{1,0:T(8,128)} async-done(((f32[1024,2048]{1,0:T(8,128)}), f32[128,2048]{1,0:T(8,128)}) %reduce-scatter.2.cloned.1.call-update) | async-done | bytes 1048592 | tf_op jit(solution)/shard_map/reduce_scatter | solution.py:55
  322.7 2.1 fusion.34
  (7 shorter events, 0.0 us)
Async XLA Ops:
  7.2 79.2 %copy-start = (bf16[1,2048,384]{2,1,0:T(8,128)(2,1)S(1)}, bf16[1,2048,384]{2,1,0:T(8,128)(2,1)}, u32[]{:S(2)}) copy-start(bf16[1,2048,384]{2,1,0:T(8,128)(2,1)} %param.11) | copy-start | bytes 4718596
  7.2 79.2 %all-gather.9.cloned.1.call-start = ((), (), s32[]{:S(2)}) async-start(), calls=%async_computation.3 | async-start | bytes 4718592 | tf_op jit(solution)/shard_map/all_gather | solution.py:44
  7.9 152.9 %all-gather.7.cloned.1.call-start = ((), (), s32[]{:S(2)}) async-start(), calls=%async_computation.2 | async-start | bytes 4718592 | tf_op jit(solution)/shard_map/all_gather | solution.py:45
  8.0 9.5 %collective-permute-start = (bf16[1,128,2048]{2,1,0:T(8,128)(2,1)}, bf16[1,128,2048]{2,1,0:T(8,128)(2,1)S(1)}, u32[]{:S(2)}, u32[]{:S(2)}) collective-permute-start(bf16[1,128,2048]{2,1,0:T(8,128)(2,1)} %param.7), channel_id=1, source_target_pairs={{0,24},{8,0},{16,8},{24,16},{1,25},{9,1},{17,9},{25,17},{2,26},{10... | collective-permute-start | bytes 1572872 | tf_op jit(solution)/shard_map/ppermute | solution.py:10
  17.4 0.8 copy-start.1
  18.3 304.5 %reduce-scatter.2.cloned.1.call-start = ((), (), s32[]{:S(2)}) async-start(), calls=%async_computation.1 | async-start | bytes 9437184 | tf_op jit(solution)/shard_map/reduce_scatter | solution.py:55
  56.4 35.9 %copy-start.3 = (bf16[1,2048,384]{2,1,0:T(8,128)(2,1)S(1)}, bf16[1,2048,384]{2,1,0:T(8,128)(2,1)}, u32[]{:S(2)}) copy-start(bf16[1,2048,384]{2,1,0:T(8,128)(2,1)} %param.12) | copy-start | bytes 4718596
  86.4 5.8 %copy-start.6 = (bf16[1,1024,2048]{2,1,0:T(8,128)(2,1)S(1)}, bf16[1,1024,2048]{2,1,0:T(8,128)(2,1)}, u32[]{:S(2)}) copy-start(bf16[1,1024,2048]{2,1,0:T(8,128)(2,1)} %all-gather.9.cloned.1.call-done) | copy-start | bytes 12582916
  167.2 2.4 copy-start.4
  167.2 2.4 copy-start.5
  187.1 135.6 %copy-start.2 = (bf16[1,128,2048]{2,1,0:T(8,128)(2,1)S(1)}, bf16[1,128,2048]{2,1,0:T(8,128)(2,1)}, u32[]{:S(2)}) copy-start(bf16[1,128,2048]{2,1,0:T(8,128)(2,1)} %copy-done.1) | copy-start | bytes 1572868
Sparse Core Ops, SparseCore 0:
  10.1 76.2 all-gather.8
  89.1 71.6 all-gather.6
  175.4 147.3 reduce-scatter.1
where the time goes:
time: 332 us; the launch traced here: 331 us
  waiting for transfers between devices  232 us (70%)
  matrix products  38.7 us (12%)
  blocking collectives  38 us (11%)
  between operations  13.8 us (4%)
  local copies, waits for them, and re-layouts  4.15 us (1%)
    reduce_scatter x1, waiting for transfers between devices, shards(): lax.psum_scatter(d_in.astype(jnp.float32), 'expert', scatter_dimension=0,...  129 us
    all_gather x1, waiting for transfers between devices, shards(): all_grads = lax.all_gather(received, 'expert', axis=0, tiled=True)  65.1 us
    all_gather x1, waiting for transfers between devices, shards(): all_tokens = lax.all_gather(tokens, 'expert', axis=0, tiled=True)  30 us
    all_gather x1, blocking collectives, shards(): all_routes = lax.all_gather(routes[0], 'expert', axis=0, tiled=True)  21.2 us
    all_gather x1, blocking collectives, shards(): all_units = lax.all_gather(gate_units[0], 'expert', axis=0, tiled=True)  16.8 us
    ppermute x1, waiting for transfers between devices, passed_along(): return lax.ppermute(value, axis, pairs)  7.02 us
  transfers between devices with their start and end apart: 4, of which 4 were waited for; matrix products, arithmetic and copies ran while one was open for 8% of the time, Pallas kernels for 0%

commit v1 on v0

--- a/solution.py
+++ b/solution.py
@@ -41,8 +41,11 @@
     received = passed_along(upstream, "section", -1)[0]
     tokens = layer_input[0]
     expert = lax.axis_index("expert") // 2
-    all_tokens = lax.all_gather(tokens, "expert", axis=0, tiled=True)
-    all_grads = lax.all_gather(received, "expert", axis=0, tiled=True)
+    all_tokens, all_grads = jnp.split(
+        lax.all_gather(jnp.concatenate([tokens, received], axis=1), "expert", axis=0, tiled=True),
+        [tokens.shape[1]],
+        axis=1,
+    )
     all_routes = lax.all_gather(routes[0], "expert", axis=0, tiled=True)
     all_units = lax.all_gather(gate_units[0], "expert", axis=0, tiled=True)
     gains = jnp.sum(

time: 332 us -> 321 us (0.967)
  matrix products: 38.7 us -> 33.3 us
  waiting for transfers between devices: 232 us -> 228 us
  local copies, waits for them, and re-layouts: 4.15 us -> 0.52 us
    all_gather x2 -> x1, waiting for transfers between devices: 95.1 us -> 89 us  [shards(): lax.all_gather(jnp.concatenate([tokens, received], axis=1), 'expert', axi...]
    unnamed x16 -> x26, local copies, waits for them, and re-layouts: 4.15 us -> 0.52 us
    dot_general x1, matrix products: 6.38 us -> 2.9 us  [expert_half(): lax.dot_general(grads, w_down, (((1,), (1,)), ((), ())), preferred_elemen...]
  transfers between devices with their start and end apart: 4 -> 3, of which waited for: 4 -> 3; matrix products, arithmetic and copies ran while one was open for 8% -> 5% of each run, Pallas kernels for 0% -> 0%
where the time goes in v1:
time: 321 us; the launch traced here: 320 us
  waiting for transfers between devices  228 us (71%)
  blocking collectives  37.7 us (12%)
  matrix products  33.3 us (10%)
  between operations  14.2 us (4%)
  other arithmetic  4.28 us (1%)
    reduce_scatter x1, waiting for transfers between devices, shards(): lax.psum_scatter(d_in.astype(jnp.float32), 'expert', scatter_dimension=0,...  132 us
    all_gather x1, waiting for transfers between devices, shards(): lax.all_gather(jnp.concatenate([tokens, received], axis=1), 'expert', axi...  89 us
    all_gather x1, blocking collectives, shards(): all_routes = lax.all_gather(routes[0], 'expert', axis=0, tiled=True)  21 us
    all_gather x1, blocking collectives, shards(): all_units = lax.all_gather(gate_units[0], 'expert', axis=0, tiled=True)  16.6 us
    ppermute x1, waiting for transfers between devices, passed_along(): return lax.ppermute(value, axis, pairs)  7.02 us
  transfers between devices with their start and end apart: 3, of which 3 were waited for; matrix products, arithmetic and copies ran while one was open for 5% of the time, Pallas kernels for 0%

profile of v1, /device:TPU:0, one launch (start us, length us, event | category | flops | bytes accessed | tf_op | source)
XLA Modules:
  0.0 320.4 jit_solution(10513925205494376032)
XLA Ops:
  7.2 0.0 copy-start
  7.2 0.0 all-gather.4.cloned.1.call-start
  7.2 2.5 collective-permute-start
  9.7 7.0 %collective-permute-done = bf16[1,128,2048]{2,1,0:T(8,128)(2,1)S(1)} collective-permute-done((bf16[1,128,2048]{2,1,0:T(8,128)(2,1)}, bf16[1,128,2048]{2,1,0:T(8,128)(2,1)S(1)}, u32[]{:S(2)}, u32[]{:S(2)}) %collective-permute-start) | collective-permute-done | bytes 524320 | tf_op jit(solution)/shard_map/ppermute | solution.py:10
  16.7 2.1 pad_maximum_fusion
  18.8 0.0 all-gather.4.cloned.1.call-update
  18.9 0.0 reduce-scatter.2.cloned.1.call-start
  18.9 0.0 copy-done.3
  18.9 21.0 %all-gather = s32[1,1024,2]{1,2,0:T(2,128)S(1)} all-gather(s32[1,128,2]{1,2,0:T(2,128)S(1)} %copy-done.3), channel_id=2, replica_groups=mesh['section'=4,'expert'=8] {'expert'}, dimensions={1}, use_global_device_ids=true | all-gather | bytes 9216 | tf_op jit(solution)/shard_map/all_gather | solution.py:49
  39.9 0.0 copy-done.4
  40.0 16.6 %all-gather.1 = s32[1,1024,2]{1,2,0:T(2,128)S(1)} all-gather(s32[1,128,2]{1,2,0:T(2,128)S(1)} %copy-done.4), channel_id=3, replica_groups=mesh['section'=4,'expert'=8] {'expert'}, dimensions={1}, use_global_device_ids=true | all-gather | bytes 9216 | tf_op jit(solution)/shard_map/all_gather | solution.py:50
  56.6 89.0 %all-gather.4.cloned.1.call-done = bf16[1024,4096]{1,0:T(8,128)(2,1)} async-done(((bf16[128,4096]{1,0:T(8,128)(2,1)}), bf16[1024,4096]{1,0:T(8,128)(2,1)}) %all-gather.4.cloned.1.call-update) | async-done | bytes 8388624 | tf_op jit(solution)/shard_map/all_gather | solution.py:45
  145.6 0.0 copy-done
  145.6 4.7 %fusion.3 = f32[1024,384]{1,0:T(8,128)S(1)} fusion(bf16[1024,4096]{1,0:T(8,128)(2,1)} %all-gather.4.cloned.1.call-done, bf16[1,2048,384]{2,1,0:T(8,128)(2,1)S(1)} %copy-done), kind=kOutput, calls=%fused_computation.8 | convolution fusion | flops 1610612736 | bytes 7340032 | tf_op jit(solution)/shard_map/dot_general | solution.py:14
  150.3 0.0 copy-done.1
  150.3 0.5 copy-done.5
  150.8 2.3 fusion.5
  153.1 0.0 copy-start.9
  153.1 2.9 multiply_convert_fusion.2
  156.0 0.0 copy-done.9
  156.0 0.0 copy-start.2
  156.0 2.4 fusion.14
  158.4 0.0 copy-done.2
  158.4 5.6 %fusion = f32[1024,2048]{1,0:T(8,128)} fusion(f32[1024,2048]{1,0:T(8,128)S(1)} %fusion.14, bf16[1024,384]{1,0:T(8,128)(2,1)S(1)} %get-tuple-element.4, bf16[1,2048,384]{2,1,0:T(8,128)(2,1)S(1)} %copy-done.1), kind=kOutput, calls=%fused_computation.2 | convolution fusion | flops 1616904192 | bytes 19136512 | tf_op jit(solution)/shard_map/dot_general | solution.py:26
  164.0 0.0 reduce-scatter.2.cloned.1.call-update
  164.1 0.0 slice-start
  164.1 6.1 %fusion.10 = bf16[1,2048,384]{2,1,0:T(8,128)(2,1)} fusion(bf16[1024,384]{1,0:T(8,128)(2,1)} %copy-done.2, bf16[1024,4096]{1,0:T(8,128)(2,1)} %all-gather.4.cloned.1.call-done), kind=kOutput, calls=%fused_computation.13 | convolution fusion | flops 1611399168 | bytes 6553600 | tf_op jit(solution)/shard_map/dot_general | solution.py:34
  170.2 6.1 %fusion.7 = bf16[1,2048,384]{2,1,0:T(8,128)(2,1)} fusion(bf16[1024,384]{1,0:T(8,128)(2,1)S(1)} %get-tuple-element.5, bf16[1024,4096]{1,0:T(8,128)(2,1)} %all-gather.4.cloned.1.call-done), kind=kOutput, calls=%fused_computation.12 | convolution fusion | flops 1611399168 | bytes 6553600 | tf_op jit(solution)/shard_map/dot_general | solution.py:31
  176.3 0.0 slice-done.1
  176.3 3.2 %fusion.13 = bf16[1,384,2048]{2,1,0:T(8,128)(2,1)} fusion(bf16[1024,4096]{1,0:T(8,128)(2,1)S(1)} %bitcast.33, f32[1024]{0:T(1024)S(1)} %fusion.24, f32[1024,384]{1,0:T(8,128)S(1)} %copy-done.10, f32[1024,384]{1,0:T(8,128)S(1)} %copy-done.8), kind=kOutput, calls=%fused_computation.14 | convolution fusion | flops 1620049920 | bytes 8916992 | tf_op jit(solution)/shard_map/dot_general | solution.py:28
  179.5 131.9 %reduce-scatter.2.cloned.1.call-done = f32[128,2048]{1,0:T(8,128)} async-done(((f32[1024,2048]{1,0:T(8,128)}), f32[128,2048]{1,0:T(8,128)}) %reduce-scatter.2.cloned.1.call-update) | async-done | bytes 1048592 | tf_op jit(solution)/shard_map/reduce_scatter | solution.py:58
  311.4 2.1 fusion.22
  (16 shorter events, 0.0 us)
Async XLA Ops:
  7.2 138.4 %copy-start = (bf16[1,2048,384]{2,1,0:T(8,128)(2,1)S(1)}, bf16[1,2048,384]{2,1,0:T(8,128)(2,1)}, u32[]{:S(2)}) copy-start(bf16[1,2048,384]{2,1,0:T(8,128)(2,1)} %param.11) | copy-start | bytes 4718596
  7.2 138.4 %all-gather.4.cloned.1.call-start = ((), (), s32[]{:S(2)}) async-start(), calls=%async_computation.1 | async-start | bytes 9437184 | tf_op jit(solution)/shard_map/all_gather | solution.py:45
  7.2 9.5 %collective-permute-start = (bf16[1,128,2048]{2,1,0:T(8,128)(2,1)}, bf16[1,128,2048]{2,1,0:T(8,128)(2,1)S(1)}, u32[]{:S(2)}, u32[]{:S(2)}) collective-permute-start(bf16[1,128,2048]{2,1,0:T(8,128)(2,1)} %param.7), channel_id=1, source_target_pairs={{0,24},{8,0},{16,8},{24,16},{1,25},{9,1},{17,9},{25,17},{2,26},{10... | collective-permute-start | bytes 1572872 | tf_op jit(solution)/shard_map/ppermute | solution.py:10
  16.7 2.2 copy-start.3
  16.7 23.2 %copy-start.4 = (s32[1,128,2]{1,2,0:T(2,128)S(1)}, s32[1,128,2]{1,2,0:T(2,128)}, u32[]{:S(2)}) copy-start(s32[1,128,2]{1,2,0:T(2,128)} %param.10) | copy-start | bytes 3076
  18.9 292.6 %reduce-scatter.2.cloned.1.call-start = ((), (), s32[]{:S(2)}) async-start(), calls=%async_computation.2 | async-start | bytes 9437184 | tf_op jit(solution)/shard_map/reduce_scatter | solution.py:58
  145.6 4.7 %copy-start.1 = (bf16[1,2048,384]{2,1,0:T(8,128)(2,1)S(1)}, bf16[1,2048,384]{2,1,0:T(8,128)(2,1)}, u32[]{:S(2)}) copy-start(bf16[1,2048,384]{2,1,0:T(8,128)(2,1)} %param.12) | copy-start | bytes 4718596
  145.6 5.1 %copy-start.5 = (bf16[1024,4096]{1,0:T(8,128)(2,1)S(1)}, bf16[1024,4096]{1,0:T(8,128)(2,1)}, u32[]{:S(2)}) copy-start(bf16[1024,4096]{1,0:T(8,128)(2,1)} %all-gather.4.cloned.1.call-done) | copy-start | bytes 25165828
  150.7 2.3 copy-start.7
  150.7 2.3 copy-start.6
  153.1 2.9 copy-start.9
  156.0 2.4 copy-start.2
  164.1 12.2 %slice-start = ((s8[8388608]{0:T(1024)(128)(4,1)}), s8[4194304]{0:T(1024)(128)(4,1)S(1)}, s32[]{:S(2)}) async-start(s8[8388608]{0:T(1024)(128)(4,1)} %bitcast.32), calls=%async_computation.3 | async-start | bytes 8388608
  170.2 6.1 %slice-start.1 = ((s8[8388608]{0:T(1024)(128)(4,1)}), s8[4194304]{0:T(1024)(128)(4,1)S(1)}, s32[]{:S(2)}) async-start(s8[8388608]{0:T(1024)(128)(4,1)} %bitcast.32), calls=%async_computation.4 | async-start | bytes 8388608
  170.2 6.1 %copy-start.8 = (f32[1024,384]{1,0:T(8,128)S(1)}, f32[1024,384]{1,0:T(8,128)}, u32[]{:S(2)}) copy-start(f32[1024,384]{1,0:T(8,128)} %copy-done.7) | copy-start | bytes 4718596
  170.2 6.1 %copy-start.10 = (f32[1024,384]{1,0:T(8,128)S(1)}, f32[1024,384]{1,0:T(8,128)}, u32[]{:S(2)}) copy-start(f32[1024,384]{1,0:T(8,128)} %copy-done.9) | copy-start | bytes 4718596
Sparse Core Ops, SparseCore 0:
  19.0 126.5 all-gather.3
  164.2 147.1 reduce-scatter.1
